TPU v7x, 256 devices: a whole 4x4x8 slice. The times are simulated.
256 devices in a mesh: row: 8 (over z), col: 32 (over y, x, core).
Axes of the slice: x: 4, y: 4, z: 8, core: 2. Of those that a mesh axis runs over, the one named last changes fastest.
Arguments:
- hidden_in: bfloat16 [1024, 2304], P('row', 'col'), may hold values from -40 to 40
- attn_gain: float32 [2304], P('col'), may hold values from 0.1 to 1.9
- qkv_weight: bfloat16 [2304, 6912], P('col'), may hold values from -0.125 to 0.125
- out_weight: bfloat16 [2304, 2304], P(None, 'col'), may hold values from -0.125 to 0.125
- moe_gain: float32 [2304], P('col'), may hold values from 0.1 to 1.9
- router_weight: float32 [2304, 8], P('col'), may hold values from -0.125 to 0.125
- expert_gate: bfloat16 [8, 2304, 5760], P('row', None, 'col'), may hold values from -0.125 to 0.125
- expert_up: bfloat16 [8, 2304, 5760], P('row', None, 'col'), may hold values from -0.125 to 0.125
- expert_down: bfloat16 [8, 5760, 2304], P('row', 'col'), may hold values from -0.078125 to 0.078125
- cache_keys: bfloat16 [2048, 64, 2304], P(('row', 'col')), may hold values from -400 to 400
- cache_values: bfloat16 [2048, 64, 2304], P(('row', 'col')), may hold values from -12 to 12
- block_table: int32 [8, 4, 64], P('row'), may hold values from 0 to 2047, as said below
- prefix_lengths: int32 [8, 4], P('row'), may hold values from 1024 to 4096, as said below
- prompt_lengths: int32 [8, 4], P('row'), may hold values from 1 to 64, 128 in all within a row
- routed_experts: int32 [1024, 2], P('row'), may hold values from 0 to 7, all different within a row; in each aligned block of 128 rows (0 to 127, 128 to 255, ...) at most 64 rows name the same one
Outputs:
- attn_out: bfloat16 [1024, 2304], P('row', 'col')
- moe_out: bfloat16 [1024, 2304], P('row', 'col')
- layer_out: bfloat16 [1024, 2304], P('row', 'col')
Inputs may be any that keep to these rules, and one draw needn't show every extreme that they name: `block_table`: entry [g, q, j] lies among the 8 pages that begin at (g * 32 + j % 32) * 8; the entries that fall among the same 8 pages are distinct. `prefix_lengths`: some request has exactly 4096 cached tokens. `prompt_lengths`: the 4 lengths of a group sum to 128; the longest of each group is exactly 64. `routed_experts`: the 2 experts of a token differ; among the tokens of one group no expert is named more than 64 times, and in some group an expert reaches 64; every expert is named by some token.
All inputs are finite; a program needn't handle non-finite values.
Results may differ from a plain program's by a relative error of at most 0.02.
The roundings to bfloat16 on the way count: a program that leaves them out, or rounds other values in their place, can miss the bound.
Values may be sent and summed in bfloat16 or wider, within the bound.
No kernel may reach another device: no remote copies, remote signals or barrier semaphores. Data moves between devices by JAX's collectives and lax.ppermute only.
A program may use at most 192 MiB of HBM per device.

v0:
```python
import math
import jax
import jax.numpy as jnp
from jax import lax
from jax.sharding import PartitionSpec as P

D = 2304
HEAD_DIM = 64
TOP = 2
norm_epsilon = 1e-05
residual_scale = 1.4 / math.sqrt(40.0)
rotary_base = 10000.0
masked_score = -1e30


def merged(value, axis, join):
    pieces = jax.tree.map(lambda part: lax.all_gather(part, axis), value)
    head = jax.tree.map(lambda part: part[0], pieces)
    tail = jax.tree.map(lambda part: part[1:], pieces)
    running, _ = lax.scan(lambda running, slab: (join(running, slab), None), head, tail)
    return running


def rotate(values, positions, head_dim):
    row_count = values.shape[0]
    head_count = values.shape[1] // head_dim
    half_dim = head_dim // 2
    frequency = rotary_base ** (-2.0 * jnp.arange(half_dim, dtype=jnp.float32) / head_dim)
    angles = positions.astype(jnp.float32)[:, None] * frequency[None, :]
    cosine = jnp.cos(angles)[:, None, :]
    sine_part = jnp.sin(angles)[:, None, :]
    shaped = values.reshape(row_count, head_count, head_dim)
    first_half = shaped[:, :, :half_dim]
    second_half = shaped[:, :, half_dim:]
    turned = jnp.concatenate(
        [
            first_half * cosine - second_half * sine_part,
            second_half * cosine + first_half * sine_part,
        ],
        axis=2,
    )
    return turned.reshape(row_count, head_count * head_dim)


def token_layout(prompt_row, prefix_row, row_count):
    run_ends = jnp.cumsum(prompt_row, dtype=jnp.int32)
    starts = run_ends - prompt_row
    offsets = jnp.arange(row_count, dtype=jnp.int32)
    request = jnp.sum(
        (offsets[:, None] >= run_ends[None, :]).astype(jnp.int32), axis=1, dtype=jnp.int32
    )
    member = request[:, None] == jnp.arange(prompt_row.shape[0], dtype=jnp.int32)[None, :]
    start_of = jnp.sum(jnp.where(member, starts[None, :], 0), axis=1, dtype=jnp.int32)
    prefix_of = jnp.sum(jnp.where(member, prefix_row[None, :], 0), axis=1, dtype=jnp.int32)
    return (request, prefix_of + offsets - start_of)


def rescale(summed, factor):
    group_count, row_count, feature_width = summed.shape
    group_size = factor.shape[1]
    shaped = summed.reshape(group_count, row_count, group_size, feature_width // group_size)
    shaped = shaped * jnp.transpose(factor, (0, 2, 1))[:, :, :, None]
    return shaped.reshape(group_count, row_count, feature_width)


def divide_rows(summed, total_weight):
    group_count, row_count, feature_width = summed.shape
    group_size = total_weight.shape[1]
    shaped = summed.reshape(group_count, row_count, group_size, feature_width // group_size)
    shaped = shaped / jnp.transpose(total_weight, (0, 2, 1))[:, :, :, None]
    return shaped.reshape(group_count, row_count, feature_width)


def combine_parts(earlier_part, later_part):
    largest = jnp.maximum(earlier_part[0], later_part[0])
    factor_one = jnp.exp(earlier_part[0] - largest)
    factor_two = jnp.exp(later_part[0] - largest)
    total_weight = earlier_part[1] * factor_one + later_part[1] * factor_two
    summed = rescale(earlier_part[2], factor_one) + rescale(later_part[2], factor_two)
    return (largest, total_weight, summed)


def on_device(
    hidden_in,
    attn_gain,
    qkv_weight,
    out_weight,
    moe_gain,
    router_weight,
    expert_gate,
    expert_up,
    expert_down,
    cache_keys,
    cache_values,
    block_table,
    prefix_lengths,
    prompt_lengths,
    routed_experts,
):
    col_count = lax.axis_size("col")
    row_devices = lax.axis_size("row")
    col_index = lax.axis_index("col")
    row_index = lax.axis_index("row")
    tok_rows = hidden_in.shape[0]
    feature_width = hidden_in.shape[1]
    head_total = out_weight.shape[0]
    head_count = head_total // HEAD_DIM
    key_share = tok_rows // col_count
    request, position = token_layout(prompt_lengths[0], prefix_lengths[0], tok_rows)
    own_start = col_index * key_share
    key_position = lax.dynamic_slice_in_dim(position, own_start, key_share)
    key_request = lax.dynamic_slice_in_dim(request, own_start, key_share)
    residual = hidden_in.astype(jnp.float32)
    squares = lax.psum(jnp.sum(residual * residual, axis=1), "col")
    scale_one = lax.rsqrt(squares / D + norm_epsilon)
    normed = (residual * scale_one[:, None] * attn_gain[None, :]).astype(jnp.bfloat16)
    query_part = jnp.dot(normed, qkv_weight[:, :head_total], preferred_element_type=jnp.float32)
    query_sum = lax.psum(query_part, "col")
    queries = (rotate(query_sum, position, HEAD_DIM) * HEAD_DIM ** (-0.5)).astype(jnp.bfloat16)
    key_value = lax.psum_scatter(
        jnp.dot(normed, qkv_weight[:, head_total:], preferred_element_type=jnp.float32).astype(
            jnp.bfloat16
        ),
        "col",
        scatter_dimension=0,
        tiled=True,
    ).astype(jnp.float32)
    new_keys = rotate(key_value[:, :head_total], key_position, HEAD_DIM).astype(jnp.bfloat16)
    new_values = key_value[:, head_total:].astype(jnp.bfloat16)
    pool_size = cache_keys.shape[0]
    page_size = cache_keys.shape[1]
    req_count = block_table.shape[1]
    pages_each = block_table.shape[2] // col_count
    page_table = block_table[0].reshape(req_count, pages_each, col_count)
    own_pages = lax.dynamic_slice_in_dim(page_table, col_index, 1, 2).reshape(
        req_count * pages_each
    )
    pool_offset_begin = (row_index * col_count + col_index) * pool_size
    slot_ids = jnp.arange(pool_size, dtype=jnp.int32)
    entry_ids = jnp.arange(req_count * pages_each, dtype=jnp.int32)
    slot_match = (own_pages - pool_offset_begin)[None, :] == slot_ids[:, None]
    entry_request = entry_ids // pages_each
    entry_page = entry_ids % pages_each * col_count + col_index
    slot_request = jnp.sum(
        jnp.where(slot_match, entry_request[None, :], 0), axis=1, dtype=jnp.int32
    )
    slot_page = jnp.sum(jnp.where(slot_match, entry_page[None, :], 0), axis=1, dtype=jnp.int32)
    prefix_row = prefix_lengths[0]
    slot_prefix = jnp.sum(
        jnp.where(
            slot_request[:, None] == jnp.arange(req_count, dtype=jnp.int32)[None, :],
            prefix_row[None, :],
            0,
        ),
        axis=1,
        dtype=jnp.int32,
    )
    cache_position = (
        slot_page[:, None] * page_size + jnp.arange(page_size, dtype=jnp.int32)[None, :]
    )
    cache_live = (
        (cache_position < slot_prefix[:, None]).astype(jnp.int32).reshape(pool_size * page_size)
    )
    cache_request = jnp.broadcast_to(slot_request[:, None], (pool_size, page_size)).reshape(
        pool_size * page_size
    )
    cache_mask = (request[:, None] == cache_request[None, :]) & (cache_live[None, :] > 0)
    fresh_mask = (request[:, None] == key_request[None, :]) & (
        key_position[None, :] <= position[:, None]
    )
    group_size = math.gcd(head_count, 4)
    group_count = head_count // group_size
    query_heads = queries.reshape(tok_rows, head_count, HEAD_DIM)
    cached_key_heads = cache_keys.reshape(pool_size * page_size, head_count, HEAD_DIM)
    cached_value_heads = cache_values.reshape(pool_size * page_size, head_count, HEAD_DIM)
    fresh_key_heads = new_keys.reshape(key_share, head_count, HEAD_DIM)
    fresh_value_heads = new_values.reshape(key_share, head_count, HEAD_DIM)

    def head_group(group_index):
        first_head = group_index * group_size
        query_piece = lax.dynamic_slice_in_dim(query_heads, first_head, group_size, 1)
        key_piece = lax.dynamic_slice_in_dim(cached_key_heads, first_head, group_size, 1)
        value_piece = lax.dynamic_slice_in_dim(cached_value_heads, first_head, group_size, 1)
        fresh_key_piece = lax.dynamic_slice_in_dim(fresh_key_heads, first_head, group_size, 1)
        fresh_value_piece = lax.dynamic_slice_in_dim(fresh_value_heads, first_head, group_size, 1)
        score_matrix = jnp.einsum(
            "thd,khd->htk", query_piece, key_piece, preferred_element_type=jnp.float32
        )
        score_matrix = jnp.where(cache_mask[None], score_matrix, masked_score)
        fresh_scores = jnp.einsum(
            "thd,khd->htk", query_piece, fresh_key_piece, preferred_element_type=jnp.float32
        )
        fresh_scores = jnp.where(fresh_mask[None], fresh_scores, masked_score)
        largest = jnp.maximum(jnp.max(score_matrix, axis=2), jnp.max(fresh_scores, axis=2))
        cached_exp = jnp.where(cache_mask[None], jnp.exp(score_matrix - largest[:, :, None]), 0.0)
        fresh_exp = jnp.where(fresh_mask[None], jnp.exp(fresh_scores - largest[:, :, None]), 0.0)
        total_weight = jnp.sum(cached_exp, axis=2) + jnp.sum(fresh_exp, axis=2)
        summed = jnp.einsum(
            "htk,khd->thd",
            cached_exp.astype(jnp.bfloat16),
            value_piece,
            preferred_element_type=jnp.float32,
        )
        summed = summed + jnp.einsum(
            "htk,khd->thd",
            fresh_exp.astype(jnp.bfloat16),
            fresh_value_piece,
            preferred_element_type=jnp.float32,
        )
        return (largest, total_weight, summed.reshape(tok_rows, group_size * HEAD_DIM))

    largest, total_weight, summed = lax.map(head_group, jnp.arange(group_count, dtype=jnp.int32))
    largest, total_weight, summed = merged((largest, total_weight, summed), "col", combine_parts)
    attended = divide_rows(summed, total_weight).astype(jnp.bfloat16)
    projected = jnp.einsum(
        "gtx,gxo->to",
        attended,
        out_weight.reshape(group_count, group_size * HEAD_DIM, feature_width),
        preferred_element_type=jnp.float32,
    )
    attn_out = projected.astype(jnp.bfloat16)
    middle = (residual + residual_scale * attn_out.astype(jnp.float32)).astype(jnp.bfloat16)
    middle_wide = middle.astype(jnp.float32)
    squares_two = lax.psum(jnp.sum(middle_wide * middle_wide, axis=1), "col")
    scale_two = lax.rsqrt(squares_two / D + norm_epsilon)
    moe_normed_f = middle_wide * scale_two[:, None] * moe_gain[None, :]
    logits = lax.psum(jnp.dot(moe_normed_f, router_weight, precision=lax.Precision.HIGHEST), "col")
    moe_normed = moe_normed_f.astype(jnp.bfloat16)
    expert_local = expert_gate.shape[0]
    expert_total = expert_local * row_devices
    capacity = 2 * TOP * tok_rows // expert_total
    onehot_three = (
        routed_experts[:, :, None] == jnp.arange(expert_total, dtype=jnp.int32)[None, None, :]
    )
    selected_logits = jnp.sum(jnp.where(onehot_three, logits[:, None, :], 0.0), axis=2)
    first_gate = jax.nn.sigmoid(selected_logits[:, 0] - selected_logits[:, 1])
    gate_pair = jnp.stack([first_gate, 1.0 - first_gate], axis=1)
    onehot = onehot_three.astype(jnp.int32).reshape(tok_rows * TOP, expert_total)
    earlier = jnp.cumsum(onehot, axis=0, dtype=jnp.int32) - onehot
    slot_index = jnp.sum(earlier * onehot, axis=1, dtype=jnp.int32)
    target = routed_experts.reshape(tok_rows * TOP) * capacity + slot_index
    token_local = jnp.arange(tok_rows * TOP, dtype=jnp.int32) // TOP
    source = jnp.zeros((expert_total * capacity,), jnp.int32).at[target].set(token_local)
    filled = jnp.zeros((expert_total * capacity,), jnp.int32).at[target].set(1)
    outgoing = jnp.where(
        filled[:, None] > 0, moe_normed[source], jnp.zeros((), jnp.bfloat16)
    ).reshape(expert_total, capacity, feature_width)
    arrived = lax.all_to_all(outgoing, "row", split_axis=0, concat_axis=0, tiled=True)
    expert_rows = (
        arrived.reshape(row_devices, expert_local, capacity, feature_width)
        .transpose(1, 0, 2, 3)
        .reshape(expert_local, row_devices * capacity, feature_width)
    )
    feature_piece = lax.all_gather(expert_rows, "col", axis=2, tiled=True)
    gate_next = jnp.einsum(
        "erd,edf->erf", feature_piece, expert_gate, preferred_element_type=jnp.float32
    )
    up_next = jnp.einsum(
        "erd,edf->erf", feature_piece, expert_up, preferred_element_type=jnp.float32
    )
    hidden = (jax.nn.silu(gate_next) * up_next).astype(jnp.bfloat16)
    received_rows = hidden.shape[1]
    value_partial_sum = jnp.einsum(
        "efo,erf->oer", expert_down, hidden, preferred_element_type=jnp.float32
    )
    expert_out = lax.psum_scatter(
        value_partial_sum.reshape(
            lax.axis_size("col") * feature_width, expert_local * received_rows
        ).astype(jnp.bfloat16),
        "col",
        scatter_dimension=0,
        tiled=True,
    )
    returned = lax.all_to_all(
        expert_out.reshape(feature_width, expert_local, received_rows),
        "row",
        split_axis=2,
        concat_axis=1,
        tiled=True,
    )
    flat_back = returned.reshape(feature_width, expert_total * capacity)
    picked = (
        jnp.take(flat_back, target, axis=1)
        .astype(jnp.float32)
        .reshape(feature_width, tok_rows, TOP)
    )
    moe_columns = jnp.sum(picked * gate_pair[None, :, :], axis=2).astype(jnp.bfloat16)
    moe_out = moe_columns.T
    layer_out = (middle_wide + residual_scale * moe_out.astype(jnp.float32)).astype(jnp.bfloat16)
    return (attn_out, moe_out, layer_out)


def solution(mesh):
    in_specs = (
        P("row", "col"),
        P("col"),
        P("col", None),
        P(None, "col"),
        P("col"),
        P("col", None),
        P("row", None, "col"),
        P("row", None, "col"),
        P("row", "col", None),
        P(("row", "col"), None, None),
        P(("row", "col"), None, None),
        P("row", None, None),
        P("row", None),
        P("row", None),
        P("row", None),
    )
    out_specs = (P("row", "col"), P("row", "col"), P("row", "col"))
    return jax.shard_map(
        on_device, mesh=mesh, in_specs=in_specs, out_specs=out_specs, check_vma=False
    )
```

profile of v0, /device:TPU:2, one launch (start us, length us, event | category | flops | bytes accessed | tf_op | source)
XLA Modules:
  0.0 942.3 jit_solution(6926186442801343392)
XLA Ops:
  8.0 62.3 %psum.28 = f32[128]{0:T(128)S(1)} all-reduce(f32[128]{0:T(128)S(1)} %fusion.64), channel_id=1, replica_groups=mesh['row'=8,'col'=32] {'col'}, use_global_device_ids=true, to_apply=%region_1.2 | all-reduce | flops 128 | bytes 1024 | tf_op jit(solution)/shard_map/psum | solution.py:114
  70.3 2.7 convolution_convert_fusion
  73.2 2.6 fusion.61
  77.7 5.0 reshape.454
  82.7 6.9 copy.162
  89.5 5.0 reshape.455
  94.5 6.7 copy.163
  102.5 88.4 %all-reduce.6.cloned.1.call-done = bf16[128,4608]{1,0:T(8,128)(2,1)} async-done(((bf16[128,4608]{1,0:T(8,128)(2,1)}), bf16[128,4608]{1,0:T(8,128)(2,1)}) %all-reduce.6.cloned.1.call-update) | async-done | bytes 1179664
  192.2 117.1 %all-reduce.4.cloned.1.call-done = f32[128,36,64]{0,2,1:T(8,128)} async-done(((f32[128,36,64]{0,2,1:T(8,128)}), f32[128,36,64]{0,2,1:T(8,128)}) %all-reduce.4.cloned.1.call-update) | async-done | bytes 1179664 | tf_op jit(solution)/shard_map/psum | solution.py:118
  309.3 1.4 multiply_subtract_fusion
  310.9 51.9 %while.31 = (s32[]{:T(128)}, f32[9,4,128]{2,1,0:T(4,128)S(1)}, f32[9,4,128]{2,1,0:T(4,128)S(1)}, f32[9,128,256]{2,1,0:T(8,128)}, s32[9]{0:T(128)S(1)}, /*index=5...) while((s32[]{:T(128)}, f32[9,4,128]{2,1,0:T(4,128)S(1)}, ...), condition=%wide.region_16.17_spmd.clone.clone, body=%wide.region_11.16_spmd.clone.clone.sunk | while | flops 69911040 | bytes 5058339 | solution.py:212
  312.5 1.4 fusion.116
  318.3 1.4 fusion.116
  335.6 1.4 fusion.116
  365.1 1.4 scatter_custom_fusion.1
  366.5 1.4 scatter_custom_fusion
  368.0 24.4 %all-gather = f32[288,4,128]{2,1,0:T(4,128)S(1)} all-gather(f32[9,4,128]{2,1,0:T(4,128)S(1)} %get-tuple-element.105), channel_id=2, replica_groups=mesh['row'=8,'col'=32] {'col'}, dimensions={0}, use_global_device_ids=true | all-gather | bytes 608256 | tf_op jit(solution)/shard_map/all_gather | solution.py:17
  392.5 25.6 %all-gather.1 = f32[288,4,128]{2,1,0:T(4,128)S(1)} all-gather(f32[9,4,128]{2,1,0:T(4,128)S(1)} %get-tuple-element.106), channel_id=3, replica_groups=mesh['row'=8,'col'=32] {'col'}, dimensions={0}, use_global_device_ids=true | all-gather | bytes 608256 | tf_op jit(solution)/shard_map/all_gather | solution.py:17
  418.2 76.0 %all-gather.8.cloned.1.call-done = f32[288,128,256]{2,1,0:T(8,128)} async-done(((f32[9,128,256]{2,1,0:T(8,128)}), f32[288,128,256]{2,1,0:T(8,128)}) %all-gather.8.cloned.1.call-update) | async-done | bytes 37748752 | tf_op jit(solution)/shard_map/all_gather | solution.py:17
  496.8 26.9 %slice.93 = f32[279,128,256]{2,1,0:T(8,128)} slice(f32[288,128,256]{2,1,0:T(8,128)} %all-gather.8.cloned.1.call-done), slice={[9:288], [0:128], [0:256]} | slice | bytes 73138176 | tf_op jit(solution)/shard_map/slice | solution.py:19
  523.7 168.2 %while.30 = (s32[]{:T(128)}, f32[9,4,128]{2,1,0:T(4,128)S(1)}, f32[9,4,128]{2,1,0:T(4,128)S(1)}, f32[9,128,256]{1,2,0:T(8,128)}, f32[31,9,4,128]{3,2,1,0:T(4,128...) while((s32[]{:T(128)}, f32[9,4,128]{2,1,0:T(4,128)S(1)}, ...), condition=%wide.region_18.19_spmd, body=%wide.region_17.18_spmd.sunk | while | flops 916994 | bytes 17676496 | solution.py:20
  526.5 2.6 fusion.111
  531.9 2.6 fusion.111
  537.4 2.6 fusion.111
  542.8 2.6 fusion.111
  548.2 2.6 fusion.111
  553.6 2.6 fusion.111
  559.1 2.6 fusion.111
  564.5 2.6 fusion.111
  569.9 2.6 fusion.111
  575.3 2.6 fusion.111
  580.8 2.6 fusion.111
  586.2 2.6 fusion.111
  591.6 2.6 fusion.111
  597.0 2.6 fusion.111
  602.5 2.6 fusion.111
  607.9 2.6 fusion.111
  613.3 2.6 fusion.111
  618.7 2.6 fusion.111
  624.2 2.6 fusion.111
  629.6 2.6 fusion.111
  635.0 2.6 fusion.111
  640.4 2.6 fusion.111
  645.9 2.6 fusion.111
  651.3 2.6 fusion.111
  656.7 2.6 fusion.111
  662.2 2.6 fusion.111
  667.6 2.6 fusion.111
  673.0 2.6 fusion.111
  678.4 2.6 fusion.111
  683.9 2.6 fusion.111
  689.3 2.6 fusion.111
  691.9 1.4 fusion.42
  694.2 60.6 %psum.30 = f32[128]{0:T(128)S(1)} all-reduce(f32[128]{0:T(128)S(1)} %get-tuple-element.401), channel_id=1, replica_groups=mesh['row'=8,'col'=32] {'col'}, use_global_device_ids=true, to_apply=%region_24.25 | all-reduce | flops 128 | bytes 1024 | tf_op jit(solution)/shard_map/psum | solution.py:224
  756.5 15.9 %all_to_all.14 = bf16[8,64,72]{2,1,0:T(8,128)(2,1)S(1)} all-to-all(bf16[8,64,72]{2,1,0:T(8,128)(2,1)S(1)} %broadcast_select_fusion), channel_id=1, replica_groups=mesh['row'=8,'col'=32] {'row'}, dimensions={0} | all-to-all | bytes 147456 | tf_op jit(solution)/shard_map/all_to_all | solution.py:248
  773.2 44.9 %all-gather.6.cloned.1.call-done = bf16[1,512,2304]{1,2,0:T(8,128)(2,1)} async-done(((bf16[1,512,72]{1,2,0:T(8,128)(2,1)}), bf16[1,512,2304]{1,2,0:T(8,128)(2,1)}) %all-gather.6.cloned.1.call-update) | async-done | bytes 2359312 | tf_op jit(solution)/shard_map/all_gather | solution.py:254
  818.1 3.0 fusion.36
  821.2 3.4 fusion.33
  824.6 2.5 copy.166
  827.9 60.4 %psum.31 = f32[128,8]{0,1:T(8,128)S(1)} all-reduce(f32[128,8]{0,1:T(8,128)S(1)} %fusion.70), channel_id=1, replica_groups=mesh['row'=8,'col'=32] {'col'}, use_global_device_ids=true, to_apply=%region_27.28 | all-reduce | flops 1024 | bytes 8192 | tf_op jit(solution)/shard_map/psum | solution.py:227
  888.4 25.3 %reduce-scatter.4.cloned.1.call-done = bf16[72,512]{1,0:T(8,128)(2,1)} async-done(((bf16[2304,512]{1,0:T(8,128)(2,1)}), bf16[72,512]{1,0:T(8,128)(2,1)}) %reduce-scatter.4.cloned.1.call-update) | async-done | bytes 73744
  915.4 1.5 reduce.2
  917.8 7.0 all-to-all-start.1
  925.0 8.3 all-to-all-done.1
  (655 shorter events, 145.1 us)
Async XLA Ops:
  7.2 814.0 %copy-start = (bf16[1,180,2304]{2,1,0:T(8,128)(2,1)S(1)}, bf16[1,180,2304]{2,1,0:T(8,128)(2,1)}, u32[]{:S(2)}) copy-start(bf16[1,180,2304]{2,1,0:T(8,128)(2,1)} %param.27) | copy-start | bytes 2488324
  7.2 183.7 %all-reduce.6.cloned.1.call-start = ((), (), s32[]{:S(2)}) async-start(), calls=%async_computation.7 | async-start | bytes 2359296
  70.3 2.9 copy-start.8
  70.3 2.9 copy-start.12
  73.1 2.9 copy-start.17
  73.1 3.2 copy-start.14
  73.1 3.4 copy-start.11
  73.1 4.6 copy-start.1
  73.1 236.2 %all-reduce.4.cloned.1.call-start = ((), (), s32[]{:S(2)}) async-start(), calls=%async_computation.3 | async-start | bytes 2359296 | tf_op jit(solution)/shard_map/psum | solution.py:118
  75.8 418.3 %all-gather.8.cloned.1.call-start = ((), (), s32[]{:S(2)}) async-start(), calls=%async_computation.5 | async-start | bytes 38928384 | tf_op jit(solution)/shard_map/all_gather | solution.py:17
  82.7 6.9 copy-start.2
  94.5 6.7 copy-start.18
  362.8 455.3 %all-gather.6.cloned.1.call-start = ((), (), s32[]{:S(2)}) async-start(), calls=%async_computation.4 | async-start | bytes 2433024 | tf_op jit(solution)/shard_map/all_gather | solution.py:254
  526.5 2.6 copy-start.4
  531.9 2.6 copy-start.4
  531.9 2.6 copy-start.6
  537.3 2.6 copy-start.4
  542.8 2.6 copy-start.4
  542.8 2.6 copy-start.6
  548.2 2.6 copy-start.4
  548.2 2.6 copy-start.6
  553.6 2.6 copy-start.4
  553.6 2.6 copy-start.6
  559.0 2.6 copy-start.4
  559.1 2.6 copy-start.6
  564.5 2.6 copy-start.4
  564.5 2.6 copy-start.6
  569.9 2.6 copy-start.4
  569.9 2.6 copy-start.6
  575.3 2.6 copy-start.4
  580.7 2.6 copy-start.4
  580.8 2.6 copy-start.6
  586.2 2.6 copy-start.4
  591.6 2.6 copy-start.4
  591.6 2.6 copy-start.6
  597.0 2.6 copy-start.4
  602.4 2.6 copy-start.4
  602.5 2.6 copy-start.6
  607.9 2.6 copy-start.4
  613.3 2.6 copy-start.4
  613.3 2.6 copy-start.6
  618.7 2.6 copy-start.4
  624.1 2.6 copy-start.4
  624.2 2.6 copy-start.6
  629.6 2.6 copy-start.4
  635.0 2.6 copy-start.4
  635.0 2.6 copy-start.6
  640.4 2.6 copy-start.4
  645.9 2.6 copy-start.4
  645.9 2.6 copy-start.6
  651.3 2.6 copy-start.4
  651.3 2.6 copy-start.6
  656.7 2.6 copy-start.4
  656.7 2.6 copy-start.6
  662.1 2.6 copy-start.4
  667.6 2.6 copy-start.4
  673.0 2.6 copy-start.4
  678.4 2.6 copy-start.4
  683.8 2.6 copy-start.4
  689.3 2.6 copy-start.4
  691.9 62.9 %copy-start.13 = (f32[72]{0:T(128)S(1)}, f32[72]{0:T(128)}, u32[]{:S(2)}) copy-start(f32[72]{0:T(128)} %param.23) | copy-start | bytes 868
  694.2 123.9 %copy-start.15 = (bf16[1,2304,180]{1,2,0:T(8,128)(2,1)S(1)}, bf16[1,2304,180]{1,2,0:T(8,128)(2,1)}, u32[]{:S(2)}) copy-start(bf16[1,2304,180]{1,2,0:T(8,128)(2,1)} %param.25) | copy-start | bytes 2488324
  773.1 140.5 %reduce-scatter.4.cloned.1.call-start = ((), (), s32[]{:S(2)}) async-start(), calls=%async_computation.6 | async-start | bytes 2433024
  917.8 15.5 %all-to-all-start.1 = ((bf16[8,2,2304]{2,1,0:T(2,128)(2,1)}), bf16[8,2,2304]{2,1,0:T(2,128)(2,1)S(1)}, u32[]{:S(2)}, u32[]{:S(2)}) async-start(bf16[8,2,2304]{2,1,0:T(2,128)(2,1)} %reshape.465), calls=%async_computation.1 | async-start | bytes 147456 | tf_op jit(solution)/shard_map/all_to_all | solution.py:274
  (82 other events, 100.2 us)
Sparse Core Ops, SparseCore 0:
  73.2 117.6 all-reduce.5
  194.2 115.0 all-reduce.3
  362.9 131.1 all-gather.7
  773.3 44.8 all-gather.5
  827.2 86.4 reduce-scatter.3
where the time goes:
time: 946 us; the launch traced here: 942 us
  waiting for transfers between devices  360 us (38%)
  blocking collectives  249 us (26%)
  local copies, waits for them, and re-layouts  164 us (17%)
  other arithmetic  97.8 us (10%)
  matrix products  40.8 us (4%)
  between operations  14.9 us (2%)
    psum x1, waiting for transfers between devices, on_device(): query_sum = lax.psum(query_part, 'col')  117 us
    unnamed x7, waiting for transfers between devices  114 us
    add x31, other arithmetic, combine_parts(): rescale(earlier_part[2], factor_one) + rescale(later_part[2], factor_two)  81.3 us
    all_gather x1, waiting for transfers between devices, merged(): pieces = jax.tree.map(lambda part: lax.all_gather(part, axis), value)  76 us
    psum x1, blocking collectives, on_device(): squares = lax.psum(jnp.sum(residual * residual, axis=1), 'col')  62.3 us
    psum x1, blocking collectives, on_device(): squares_two = lax.psum(jnp.sum(middle_wide * middle_wide, axis=1), 'col')  60.6 us
    psum x1, blocking collectives, on_device(): lax.psum(jnp.dot(moe_normed_f, router_weight, precision=lax.Precision.HIG...  60.4 us
    dynamic_slice x62, local copies, waits for them, and re-layouts, merged(): lax.scan(lambda running, slab: (join(running, slab), None), head, tail)  53.9 us
  transfers between devices with their start and end apart: 6, of which 6 were waited for; matrix products, arithmetic and copies ran while one was open for 4% of the time, Pallas kernels for 0%

commit v1 on v0

--- a/solution.py
+++ b/solution.py
@@ -11,6 +11,15 @@
 residual_scale = 1.4 / math.sqrt(40.0)
 rotary_base = 10000.0
 masked_score = -1e30
+
+
+def doubling_sum(x, axis):
+    size = lax.axis_size(axis)
+    total, reach = (x, 1)
+    while reach < size:
+        total = total + lax.ppermute(total, axis, [(i, i ^ reach) for i in range(size)])
+        reach = 2 * reach
+    return total
 
 
 def merged(value, axis, join):
@@ -115,7 +124,7 @@
     scale_one = lax.rsqrt(squares / D + norm_epsilon)
     normed = (residual * scale_one[:, None] * attn_gain[None, :]).astype(jnp.bfloat16)
     query_part = jnp.dot(normed, qkv_weight[:, :head_total], preferred_element_type=jnp.float32)
-    query_sum = lax.psum(query_part, "col")
+    query_sum = doubling_sum(query_part, "col")
     queries = (rotate(query_sum, position, HEAD_DIM) * HEAD_DIM ** (-0.5)).astype(jnp.bfloat16)
     key_value = lax.psum_scatter(
         jnp.dot(normed, qkv_weight[:, head_total:], preferred_element_type=jnp.float32).astype(

time: 946 us -> 893 us (0.944)
  waiting for transfers between devices: 360 us -> 294 us
    psum x1 -> x0, waiting for transfers between devices: 117 us -> none  [on_device(): query_sum = lax.psum(query_part, 'col')]
    ppermute x0 -> x5, waiting for transfers between devices: none -> 84.7 us  [doubling_sum(): lax.ppermute(total, axis, [(i, i ^ reach) for i in range(size)])]
    unnamed x7 -> x6, waiting for transfers between devices: 114 us -> 79.9 us
  transfers between devices with their start and end apart: 6 -> 10, of which waited for: 6 -> 9; matrix products, arithmetic and copies ran while one was open for 4% -> 5% of each run, Pallas kernels for 0% -> 0%
where the time goes in v1:
time: 893 us; the launch traced here: 889 us
  waiting for transfers between devices  294 us (33%)
  blocking collectives  249 us (28%)
  local copies, waits for them, and re-layouts  169 us (19%)
  other arithmetic  101 us (11%)
  matrix products  38.5 us (4%)
  between operations  14.9 us (2%)
  starting transfers between devices  13.2 us (1%)
    ppermute x5, waiting for transfers between devices, doubling_sum(): lax.ppermute(total, axis, [(i, i ^ reach) for i in range(size)])  84.7 us
    add x31, other arithmetic, combine_parts(): rescale(earlier_part[2], factor_one) + rescale(later_part[2], factor_two)  81.3 us
    unnamed x6, waiting for transfers between devices  79.9 us
    all_gather x1, waiting for transfers between devices, merged(): pieces = jax.tree.map(lambda part: lax.all_gather(part, axis), value)  76.1 us
    psum x1, blocking collectives, on_device(): squares = lax.psum(jnp.sum(residual * residual, axis=1), 'col')  62.3 us
    psum x1, blocking collectives, on_device(): squares_two = lax.psum(jnp.sum(middle_wide * middle_wide, axis=1), 'col')  60.5 us
    psum x1, blocking collectives, on_device(): lax.psum(jnp.dot(moe_normed_f, router_weight, precision=lax.Precision.HIG...  60.4 us
    dynamic_slice x62, local copies, waits for them, and re-layouts, merged(): lax.scan(lambda running, slab: (join(running, slab), None), head, tail)  53.9 us
  transfers between devices with their start and end apart: 10, of which 9 were waited for; matrix products, arithmetic and copies ran while one was open for 5% of the time, Pallas kernels for 0%

profile of v1, /device:TPU:2, one launch (start us, length us, event | category | flops | bytes accessed | tf_op | source)
XLA Modules:
  0.0 889.0 jit_solution(670525164943464244)
XLA Ops:
  8.0 62.3 %psum.21 = f32[128]{0:T(128)S(1)} all-reduce(f32[128]{0:T(128)S(1)} %fusion.64), channel_id=1, replica_groups=mesh['row'=8,'col'=32] {'col'}, use_global_device_ids=true, to_apply=%region_1.2 | all-reduce | flops 128 | bytes 1024 | tf_op jit(solution)/shard_map/psum | solution.py:123
  70.3 1.4 fusion.61
  71.8 2.8 collective-permute-done
  74.8 5.7 collective-permute-start.1
  80.5 26.3 %collective-permute-done.1 = f32[128,2304]{1,0:T(8,128)S(1)} collective-permute-done((f32[128,2304]{1,0:T(8,128)S(1)}, f32[128,2304]{1,0:T(8,128)S(1)}, u32[]{:S(2)}, u32[]{:S(2)}) %collective-permute-start.1) | collective-permute-done | bytes 1179680 | tf_op jit(solution)/shard_map/ppermute | solution.py:20
  107.1 1.6 convolution_convert_fusion
  109.5 27.7 %collective-permute-done.2 = f32[128,2304]{1,0:T(8,128)} collective-permute-done((f32[128,2304]{1,0:T(8,128)S(1)}, f32[128,2304]{1,0:T(8,128)}, u32[]{:S(2)}, u32[]{:S(2)}) %collective-permute-start.2) | collective-permute-done | bytes 1179680 | tf_op jit(solution)/shard_map/ppermute | solution.py:20
  137.3 1.5 add.212
  139.2 27.9 %collective-permute-done.3 = f32[128,2304]{1,0:T(8,128)} collective-permute-done((f32[128,2304]{1,0:T(8,128)S(1)}, f32[128,2304]{1,0:T(8,128)}, u32[]{:S(2)}, u32[]{:S(2)}) %collective-permute-start.3) | collective-permute-done | bytes 1179680 | tf_op jit(solution)/shard_map/ppermute | solution.py:20
  167.1 1.5 add.213
  169.0 7.8 reshape.454
  176.8 6.7 copy.162
  183.5 7.8 reshape.455
  191.3 6.7 copy.163
  199.5 54.5 %all-reduce.3.cloned.1.call-done = bf16[128,4608]{1,0:T(8,128)(2,1)} async-done(((bf16[128,4608]{1,0:T(8,128)(2,1)}), bf16[128,4608]{1,0:T(8,128)(2,1)}) %all-reduce.3.cloned.1.call-update) | async-done | bytes 1179664
  255.3 1.5 add.214
  257.5 51.9 %while.31 = (s32[]{:T(128)}, f32[9,4,128]{2,1,0:T(4,128)S(1)}, f32[9,4,128]{2,1,0:T(4,128)S(1)}, f32[9,128,256]{2,1,0:T(8,128)}, s32[9]{0:T(128)S(1)}, /*index=5...) while((s32[]{:T(128)}, f32[9,4,128]{2,1,0:T(4,128)S(1)}, ...), condition=%wide.region_15.16_spmd.clone.clone, body=%wide.region_10.15_spmd.clone.clone.sunk | while | flops 69911040 | bytes 5058339 | solution.py:221
  314.6 24.6 %all-gather = f32[288,4,128]{2,1,0:T(4,128)S(1)} all-gather(f32[9,4,128]{2,1,0:T(4,128)S(1)} %get-tuple-element.105), channel_id=2, replica_groups=mesh['row'=8,'col'=32] {'col'}, dimensions={0}, use_global_device_ids=true | all-gather | bytes 608256 | tf_op jit(solution)/shard_map/all_gather | solution.py:26
  339.3 25.4 %all-gather.1 = f32[288,4,128]{2,1,0:T(4,128)S(1)} all-gather(f32[9,4,128]{2,1,0:T(4,128)S(1)} %get-tuple-element.106), channel_id=3, replica_groups=mesh['row'=8,'col'=32] {'col'}, dimensions={0}, use_global_device_ids=true | all-gather | bytes 608256 | tf_op jit(solution)/shard_map/all_gather | solution.py:26
  364.8 76.1 %all-gather.8.cloned.1.call-done = f32[288,128,256]{2,1,0:T(8,128)} async-done(((f32[9,128,256]{2,1,0:T(8,128)}), f32[288,128,256]{2,1,0:T(8,128)}) %all-gather.8.cloned.1.call-update) | async-done | bytes 37748752 | tf_op jit(solution)/shard_map/all_gather | solution.py:26
  443.6 26.9 %slice.93 = f32[279,128,256]{2,1,0:T(8,128)} slice(f32[288,128,256]{2,1,0:T(8,128)} %all-gather.8.cloned.1.call-done), slice={[9:288], [0:128], [0:256]} | slice | bytes 73138176 | tf_op jit(solution)/shard_map/slice | solution.py:28
  470.5 168.2 %while.30 = (s32[]{:T(128)}, f32[9,4,128]{2,1,0:T(4,128)S(1)}, f32[9,4,128]{2,1,0:T(4,128)S(1)}, f32[9,128,256]{1,2,0:T(8,128)}, f32[31,9,4,128]{3,2,1,0:T(4,128...) while((s32[]{:T(128)}, f32[9,4,128]{2,1,0:T(4,128)S(1)}, ...), condition=%wide.region_17.18_spmd, body=%wide.region_16.17_spmd.sunk | while | flops 916994 | bytes 17676496 | solution.py:29
  473.3 2.6 fusion.111
  478.7 2.6 fusion.111
  484.1 2.6 fusion.111
  489.5 2.6 fusion.111
  495.0 2.6 fusion.111
  500.4 2.6 fusion.111
  505.8 2.6 fusion.111
  511.2 2.6 fusion.111
  516.7 2.6 fusion.111
  522.1 2.6 fusion.111
  527.5 2.6 fusion.111
  532.9 2.6 fusion.111
  538.4 2.6 fusion.111
  543.8 2.6 fusion.111
  549.2 2.6 fusion.111
  554.6 2.6 fusion.111
  560.1 2.6 fusion.111
  565.5 2.6 fusion.111
  570.9 2.6 fusion.111
  576.3 2.6 fusion.111
  581.8 2.6 fusion.111
  587.2 2.6 fusion.111
  592.6 2.6 fusion.111
  598.1 2.6 fusion.111
  603.5 2.6 fusion.111
  608.9 2.6 fusion.111
  614.3 2.6 fusion.111
  619.8 2.6 fusion.111
  625.2 2.6 fusion.111
  630.6 2.6 fusion.111
  636.0 2.6 fusion.111
  641.0 60.5 %psum.22 = f32[128]{0:T(128)S(1)} all-reduce(f32[128]{0:T(128)S(1)} %get-tuple-element.401), channel_id=1, replica_groups=mesh['row'=8,'col'=32] {'col'}, use_global_device_ids=true, to_apply=%region_23.24 | all-reduce | flops 128 | bytes 1024 | tf_op jit(solution)/shard_map/psum | solution.py:233
  703.2 15.9 %all_to_all.14 = bf16[8,64,72]{2,1,0:T(8,128)(2,1)S(1)} all-to-all(bf16[8,64,72]{2,1,0:T(8,128)(2,1)S(1)} %broadcast_select_fusion), channel_id=1, replica_groups=mesh['row'=8,'col'=32] {'row'}, dimensions={0} | all-to-all | bytes 147456 | tf_op jit(solution)/shard_map/all_to_all | solution.py:257
  719.9 44.9 %all-gather.6.cloned.1.call-done = bf16[1,512,2304]{1,2,0:T(8,128)(2,1)} async-done(((bf16[1,512,72]{1,2,0:T(8,128)(2,1)}), bf16[1,512,2304]{1,2,0:T(8,128)(2,1)}) %all-gather.6.cloned.1.call-update) | async-done | bytes 2359312 | tf_op jit(solution)/shard_map/all_gather | solution.py:263
  764.8 3.0 fusion.36
  767.9 3.4 fusion.33
  771.3 2.5 copy.166
  774.6 60.4 %psum.23 = f32[128,8]{0,1:T(8,128)S(1)} all-reduce(f32[128,8]{0,1:T(8,128)S(1)} %fusion.70), channel_id=1, replica_groups=mesh['row'=8,'col'=32] {'col'}, use_global_device_ids=true, to_apply=%region_26.27 | all-reduce | flops 1024 | bytes 8192 | tf_op jit(solution)/shard_map/psum | solution.py:236
  835.1 25.3 %reduce-scatter.4.cloned.1.call-done = bf16[72,512]{1,0:T(8,128)(2,1)} async-done(((bf16[2304,512]{1,0:T(8,128)(2,1)}), bf16[72,512]{1,0:T(8,128)(2,1)}) %reduce-scatter.4.cloned.1.call-update) | async-done | bytes 73744
  862.1 1.5 reduce.2
  864.5 7.0 all-to-all-start.1
  871.7 8.3 all-to-all-done.1
  (666 shorter events, 154.5 us)
Async XLA Ops:
  7.2 760.7 %copy-start = (bf16[1,180,2304]{2,1,0:T(8,128)(2,1)S(1)}, bf16[1,180,2304]{2,1,0:T(8,128)(2,1)}, u32[]{:S(2)}) copy-start(bf16[1,180,2304]{2,1,0:T(8,128)(2,1)} %param.27) | copy-start | bytes 2488324
  7.2 246.9 %all-reduce.3.cloned.1.call-start = ((), (), s32[]{:S(2)}) async-start(), calls=%async_computation.6 | async-start | bytes 2359296
  71.7 2.9 collective-permute-start
  74.8 32.2 %copy-start.3 = (bf16[72,6912]{1,0:T(8,128)(2,1)S(1)}, bf16[72,6912]{1,0:T(8,128)(2,1)}, u32[]{:S(2)}) copy-start(bf16[72,6912]{1,0:T(8,128)(2,1)} %param.21) | copy-start | bytes 2985988
  74.8 32.2 %copy-start.7 = (bf16[128,72]{0,1:T(8,128)(2,1)S(1)}, bf16[128,72]{0,1:T(8,128)(2,1)}, u32[]{:S(2)}) copy-start(bf16[128,72]{0,1:T(8,128)(2,1)} %param.19) | copy-start | bytes 55300
  74.8 32.2 %copy-start.11 = (f32[72]{0:T(128)S(1)}, f32[72]{0:T(128)}, u32[]{:S(2)}) copy-start(f32[72]{0:T(128)} %param.20) | copy-start | bytes 868
  74.8 31.9 %collective-permute-start.1 = (f32[128,2304]{1,0:T(8,128)S(1)}, f32[128,2304]{1,0:T(8,128)S(1)}, u32[]{:S(2)}, u32[]{:S(2)}) collective-permute-start(f32[128,2304]{1,0:T(8,128)S(1)} %add.210), channel_id=1, source_target_pairs={{0,2},{1,3},{2,0},{3,1},{4,6},{5,7},{6,4},{7,5},{8,10},{9,11},{10,... | collective-permute-start | bytes 3538952 | tf_op jit(solution)/shard_map/ppermute | solution.py:20
  106.9 30.3 %collective-permute-start.2 = (f32[128,2304]{1,0:T(8,128)S(1)}, f32[128,2304]{1,0:T(8,128)}, u32[]{:S(2)}, u32[]{:S(2)}) collective-permute-start(f32[128,2304]{1,0:T(8,128)S(1)} %add.211), channel_id=1, source_target_pairs={{0,4},{1,5},{2,6},{3,7},{4,0},{5,1},{6,2},{7,3},{8,12},{9,13},{10,... | collective-permute-start | bytes 3538952 | tf_op jit(solution)/shard_map/ppermute | solution.py:20
  108.7 332.2 %all-gather.8.cloned.1.call-start = ((), (), s32[]{:S(2)}) async-start(), calls=%async_computation.4 | async-start | bytes 38928384 | tf_op jit(solution)/shard_map/all_gather | solution.py:26
  138.7 28.4 %collective-permute-start.3 = (f32[128,2304]{1,0:T(8,128)S(1)}, f32[128,2304]{1,0:T(8,128)}, u32[]{:S(2)}, u32[]{:S(2)}) collective-permute-start(f32[128,2304]{1,0:T(8,128)S(1)} %add.212), channel_id=1, source_target_pairs={{0,8},{1,9},{2,10},{3,11},{4,12},{5,13},{6,14},{7,15},{8,0},{9,1},... | collective-permute-start | bytes 3538952 | tf_op jit(solution)/shard_map/ppermute | solution.py:20
  168.6 86.7 %collective-permute-start.4 = (f32[128,2304]{1,0:T(8,128)S(1)}, f32[128,2304]{1,0:T(8,128)}, u32[]{:S(2)}, u32[]{:S(2)}) collective-permute-start(f32[128,2304]{1,0:T(8,128)S(1)} %add.213), channel_id=1, source_target_pairs={{0,16},{1,17},{2,18},{3,19},{4,20},{5,21},{6,22},{7,23},{8,24},{9,... | collective-permute-start | bytes 3538952 | tf_op jit(solution)/shard_map/ppermute | solution.py:20
  191.3 6.7 copy-start.17
  309.4 455.4 %all-gather.6.cloned.1.call-start = ((), (), s32[]{:S(2)}) async-start(), calls=%async_computation.3 | async-start | bytes 2433024 | tf_op jit(solution)/shard_map/all_gather | solution.py:263
  473.2 2.6 copy-start.2
  478.7 2.6 copy-start.2
  478.7 2.6 copy-start.5
  484.1 2.6 copy-start.2
  489.5 2.6 copy-start.2
  489.5 2.6 copy-start.5
  494.9 2.6 copy-start.2
  500.4 2.6 copy-start.2
  500.4 2.6 copy-start.5
  505.8 2.6 copy-start.2
  511.2 2.6 copy-start.2
  511.2 2.6 copy-start.5
  516.6 2.6 copy-start.2
  522.1 2.6 copy-start.2
  522.1 2.6 copy-start.5
  527.5 2.6 copy-start.2
  532.9 2.6 copy-start.2
  532.9 2.6 copy-start.5
  538.3 2.6 copy-start.2
  543.8 2.6 copy-start.2
  543.8 2.6 copy-start.5
  549.2 2.6 copy-start.2
  549.2 2.6 copy-start.5
  554.6 2.6 copy-start.2
  554.6 2.6 copy-start.5
  560.1 2.6 copy-start.2
  560.1 2.6 copy-start.5
  565.5 2.6 copy-start.2
  565.5 2.6 copy-start.5
  570.9 2.6 copy-start.2
  570.9 2.6 copy-start.5
  576.3 2.6 copy-start.2
  581.8 2.6 copy-start.2
  581.8 2.6 copy-start.5
  587.2 2.6 copy-start.2
  592.6 2.6 copy-start.2
  592.6 2.6 copy-start.5
  598.0 2.6 copy-start.2
  603.5 2.6 copy-start.2
  603.5 2.6 copy-start.5
  608.9 2.6 copy-start.2
  614.3 2.6 copy-start.2
  614.3 2.6 copy-start.5
  619.7 2.6 copy-start.2
  625.2 2.6 copy-start.2
  630.6 2.6 copy-start.2
  636.0 2.6 copy-start.2
  638.7 62.8 %copy-start.12 = (f32[72]{0:T(128)S(1)}, f32[72]{0:T(128)}, u32[]{:S(2)}) copy-start(f32[72]{0:T(128)} %param.23) | copy-start | bytes 868
  641.0 123.9 %copy-start.14 = (bf16[1,2304,180]{1,2,0:T(8,128)(2,1)S(1)}, bf16[1,2304,180]{1,2,0:T(8,128)(2,1)}, u32[]{:S(2)}) copy-start(bf16[1,2304,180]{1,2,0:T(8,128)(2,1)} %param.25) | copy-start | bytes 2488324
  719.8 140.5 %reduce-scatter.4.cloned.1.call-start = ((), (), s32[]{:S(2)}) async-start(), calls=%async_computation.5 | async-start | bytes 2433024
  864.5 15.5 %all-to-all-start.1 = ((bf16[8,2,2304]{2,1,0:T(2,128)(2,1)}), bf16[8,2,2304]{2,1,0:T(2,128)(2,1)S(1)}, u32[]{:S(2)}, u32[]{:S(2)}) async-start(bf16[8,2,2304]{2,1,0:T(2,128)(2,1)} %reshape.465), calls=%async_computation.1 | async-start | bytes 147456 | tf_op jit(solution)/shard_map/all_to_all | solution.py:283
  (85 other events, 106.5 us)
Sparse Core Ops, SparseCore 0:
  108.8 145.1 all-reduce.2
  309.5 131.3 all-gather.7
  720.0 44.8 all-gather.5
  773.9 86.4 reduce-scatter.3
